TPU v7x, 256 devices: a whole 4x4x8 slice. The times are simulated.
256 devices in a mesh: neuron: 32 (over y, z), tm: 2 (over core), trial: 4 (over x).
Axes of the slice: x: 4, y: 4, z: 8, core: 2. Of those that a mesh axis runs over, the one named last changes fastest.
Arguments:
- tensor: bfloat16 [8192, 256, 512], P('neuron', 'tm', 'trial'), may hold values from -6 to 6
- present_blocks: int32 [64, 16], P('neuron'), may hold values 0 or 1
- trial_day: int32 [512], P('trial'), may hold values from 0 to 15
- time_factor: bfloat16 [256, 256], P('tm'), may hold values from 0 to 1
- trial_factor: bfloat16 [512, 256], P('trial'), may hold values from 0 to 1
Outputs:
- neuron_out: bfloat16 [8192, 256], P(('neuron', 'tm', 'trial'))
- time_out: bfloat16 [256, 256], P('tm')
- trial_out: bfloat16 [512, 256], P('trial')
All inputs are finite; a program needn't handle non-finite values. No bound on the sum of `present_blocks` on one device may be relied on, other than what follows from the above.
Results may differ from a plain program's by a relative error of at most 0.0051.
The roundings to bfloat16 on the way count: a program that leaves them out, or rounds other values in their place, can miss the bound.
Values may be sent and summed in bfloat16 or wider, within the bound.
No kernel may reach another device: no remote copies, remote signals or barrier semaphores. Data moves between devices by JAX's collectives and lax.ppermute only.
A program may use at most 128 MiB of HBM per device.

v0:
```python
import jax
import jax.numpy as jnp
from jax import lax
from jax.sharding import PartitionSpec as P

RIDGE = 0.1
EPSILON = 1e-06


def normal_inverse(gram_matrix):
    order_size = gram_matrix.shape[0]
    identity = jnp.eye(order_size, dtype=jnp.float32)
    scaled = gram_matrix / jnp.mean(jnp.diagonal(gram_matrix)) + RIDGE * identity
    lower_factor = jnp.linalg.cholesky(scaled)
    return jax.scipy.linalg.cho_solve((lower_factor, True), identity)


def apply_inverse(partial_sums, inverse):
    return jnp.dot(partial_sums, inverse, precision=lax.Precision.HIGHEST)


def raw_gram(raw_rows):
    return jnp.dot(raw_rows.T, raw_rows, precision=lax.Precision.HIGHEST)


def khatri_rao(left_rows, right_rows):
    return (
        left_rows.astype(jnp.float32)[:, None, :] * right_rows.astype(jnp.float32)[None, :, :]
    ).astype(jnp.bfloat16)


def rescale(raw_rows, gram_sum, total_rows):
    scales = jnp.sqrt(jnp.diagonal(gram_sum) / total_rows + EPSILON)
    factor = (raw_rows / scales[None, :]).astype(jnp.bfloat16)
    normed = gram_sum / (scales[:, None] * scales[None, :])
    return (factor, normed)


def mask_tensor(tensor, present_blocks, trial_day):
    day_count = present_blocks.shape[1]
    onehot = (trial_day[:, None] == jnp.arange(day_count, dtype=jnp.int32)[None, :]).astype(
        jnp.float32
    )
    block_mask = jnp.dot(present_blocks.astype(jnp.float32), onehot.T)
    block_count = present_blocks.shape[0]
    shaped = tensor.reshape(
        block_count, tensor.shape[0] // block_count, tensor.shape[1], tensor.shape[2]
    )
    return shaped * block_mask.astype(jnp.bfloat16)[:, None, None, :]


def factor_gram(rows):
    return jnp.dot(rows.T, rows, preferred_element_type=jnp.float32)


def on_device(tensor, present_blocks, trial_day, time_factor, trial_factor):
    time_all = lax.all_gather(time_factor, "tm", axis=0, tiled=True)
    trial_all = lax.all_gather(trial_factor, "trial", axis=0, tiled=True)
    blocks = mask_tensor(tensor, present_blocks, trial_day)
    block_count, block_rows, time_rows, trial_rows = blocks.shape
    neuron_rows = block_count * block_rows
    flattened = blocks.reshape(neuron_rows, time_rows, trial_rows)
    rank_size = time_factor.shape[1]
    start_time = factor_gram(time_all)
    start_trial = factor_gram(trial_all)
    inverse_neuron = normal_inverse(start_time * start_trial)
    kr_tk = khatri_rao(time_factor, trial_factor)
    neuron_total = neuron_rows * lax.axis_size("neuron")
    block_sums = lax.psum(
        jnp.einsum("itk,tkr->ir", flattened, kr_tk, preferred_element_type=jnp.float32),
        ("tm", "trial"),
    )
    raw_rows = apply_inverse(block_sums, inverse_neuron)
    gram_sum = lax.psum(raw_gram(raw_rows), "neuron")
    neuron_local, gram_neuron = rescale(raw_rows, gram_sum, neuron_total)
    own_rows = neuron_rows // (lax.axis_size("tm") * lax.axis_size("trial"))
    own_index = lax.axis_index("tm") * lax.axis_size("trial") + lax.axis_index("trial")
    neuron_own = lax.dynamic_slice_in_dim(neuron_local, own_index * own_rows, own_rows, axis=0)
    neuron_blocks = neuron_local.reshape(block_count, block_rows, rank_size)
    time_total = time_rows * lax.axis_size("tm")
    inverse_time = normal_inverse(gram_neuron * start_trial)

    def time_add_block(running, inputs):
        tensor_piece, rows_a = inputs
        kr_ik = khatri_rao(rows_a, trial_factor)
        return (
            running
            + jnp.einsum("itk,ikr->tr", tensor_piece, kr_ik, preferred_element_type=jnp.float32),
            None,
        )

    running, unused = lax.scan(
        time_add_block, jnp.zeros((time_rows, rank_size), jnp.float32), (blocks, neuron_blocks)
    )
    half_sums = lax.psum(running, ("neuron", "trial"))
    raw_rows = apply_inverse(half_sums, inverse_time)
    gram_sum = lax.psum(raw_gram(raw_rows), "tm")
    time_local, gram_time = rescale(raw_rows, gram_sum, time_total)
    trial_total = trial_rows * lax.axis_size("trial")
    inverse_trial = normal_inverse(gram_neuron * gram_time)

    def trial_add_block(running, inputs):
        tensor_piece, rows_a = inputs
        kr_it = khatri_rao(rows_a, time_local)
        return (
            running
            + jnp.einsum("itk,itr->kr", tensor_piece, kr_it, preferred_element_type=jnp.float32),
            None,
        )

    running, unused = lax.scan(
        trial_add_block, jnp.zeros((trial_rows, rank_size), jnp.float32), (blocks, neuron_blocks)
    )
    quarter_sums = lax.psum(running, ("neuron", "tm"))
    raw_rows = apply_inverse(quarter_sums, inverse_trial)
    squares = lax.psum(jnp.sum(raw_rows * raw_rows, axis=0), "trial")
    scales = jnp.sqrt(squares / trial_total + EPSILON)
    trial_local = (raw_rows / scales[None, :]).astype(jnp.bfloat16)
    return (neuron_own, time_local, trial_local)


def solution(mesh):
    return jax.shard_map(
        on_device,
        mesh=mesh,
        in_specs=(
            P("neuron", "tm", "trial"),
            P("neuron", None),
            P("trial"),
            P("tm", None),
            P("trial", None),
        ),
        out_specs=(P(("neuron", "tm", "trial"), None), P("tm", None), P("trial", None)),
        check_vma=False,
    )
```

profile of v0, /device:TPU:1, one launch (start us, length us, event | category | flops | bytes accessed | tf_op | source)
XLA Modules:
  0.0 862.3 jit_solution(6178857749009200221)
XLA Ops:
  9.9 7.2 broadcast_multiply_fusion.1
  17.1 9.9 %fusion.28 = f32[256,256]{1,0:T(8,128)} fusion(f32[128,256]{1,0:T(8,128)S(1)} %convert_element_type.81, f32[128,256]{1,0:T(8,128)S(1)} %convert_element_type.80, bf16[256,128,128]{2,1,0:T(8,128)(2,1)} %broadcast_multiply_fusion.1), kind=kOutput, calls=%fused_computation.39 | convolution fusion | flops 2155872256 | bytes 8912896 | tf_op jit(solution)/shard_map/itk,tkr->ir/dot_general | solution.py:70
  27.1 11.0 %all_gather.7 = bf16[512,256]{1,0:T(8,128)(2,1)S(1)} all-gather(bf16[128,256]{1,0:T(8,128)(2,1)S(1)} %copy-done.1), channel_id=1, replica_groups=mesh['neuron'=32,'tm'=2,'trial'=4] {'trial'}, dimensions={0}, use_global_device_ids=true | all-gather | bytes 327680 | tf_op jit(solution)/shard_map/all_gather | solution.py:58
  38.1 6.3 all_gather.6
  44.4 11.9 %copy.27 = bf16[256,128,128]{1,2,0:T(8,128)(2,1)} copy(bf16[256,128,128]{2,1,0:T(8,128)(2,1)} %param.12) | data formatting | bytes 16777216 | tf_op args[0]
  60.7 11.7 %cholesky.172 = f32[128,128]{1,0:T(8,128)S(1)} custom-call(f32[128,128]{1,0:T(8,128)S(1)} %cholesky.270), custom_call_target="Cholesky" | custom-call | tf_op jit(solution)/shard_map/jit(cholesky)/cholesky | solution.py:14
  72.5 9.8 %custom-call.29 = f32[1,128,128]{1,2,0:T(8,128)S(1)} custom-call(f32[1,128,128]{2,1,0:T(8,128)S(1)} %get-tuple-element.207), custom_call_target="InvertDiagBlocksLowerTriangular" | custom-call | tf_op jit(solution)/shard_map/jit(cholesky)/cholesky | solution.py:14
  82.8 11.7 %cholesky.189 = f32[128,128]{1,0:T(8,128)S(1)} custom-call(f32[128,128]{1,0:T(8,128)S(1)} %convolution_subtract_fusion.8), custom_call_target="Cholesky" | custom-call | tf_op jit(solution)/shard_map/jit(cholesky)/cholesky | solution.py:14
  96.6 4.0 while.30
  100.6 19.9 %custom-call.30 = f32[2,128,128]{1,2,0:T(8,128)S(1)} custom-call(f32[2,128,128]{2,1,0:T(8,128)S(1)} %get-tuple-element.117), custom_call_target="InvertDiagBlocksLowerTriangular" | custom-call | tf_op jit(solution)/shard_map/jit(_cho_solve)/triangular_solve | solution.py:15
  125.1 7.2 broadcast_multiply_fusion
  132.5 134.6 %all-reduce.9.cloned.1.call-done = f32[256,256]{0,1:T(8,128)} async-done(((f32[256,256]{0,1:T(8,128)}), f32[256,256]{0,1:T(8,128)}) %all-reduce.9.cloned.1.call-update) | async-done | bytes 262160 | tf_op jit(solution)/shard_map/psum | solution.py:74
  274.7 11.7 %cholesky.206 = f32[128,128]{1,0:T(8,128)S(1)} custom-call(f32[128,128]{1,0:T(8,128)S(1)} %cholesky.273), custom_call_target="Cholesky" | custom-call | tf_op jit(solution)/shard_map/jit(cholesky)/cholesky | solution.py:14
  286.5 9.8 %custom-call.31 = f32[1,128,128]{1,2,0:T(8,128)S(1)} custom-call(f32[1,128,128]{2,1,0:T(8,128)S(1)} %get-tuple-element.203), custom_call_target="InvertDiagBlocksLowerTriangular" | custom-call | tf_op jit(solution)/shard_map/jit(cholesky)/cholesky | solution.py:14
  296.8 11.7 %cholesky.223 = f32[128,128]{1,0:T(8,128)S(1)} custom-call(f32[128,128]{1,0:T(8,128)S(1)} %convolution_subtract_fusion.7), custom_call_target="Cholesky" | custom-call | tf_op jit(solution)/shard_map/jit(cholesky)/cholesky | solution.py:14
  311.0 3.8 while.31
  314.9 20.1 %custom-call.32 = f32[2,128,128]{1,2,0:T(8,128)S(1)} custom-call(f32[2,128,128]{2,1,0:T(8,128)S(1)} %get-tuple-element.118), custom_call_target="InvertDiagBlocksLowerTriangular" | custom-call | tf_op jit(solution)/shard_map/jit(_cho_solve)/triangular_solve | solution.py:15
  336.7 7.4 while.28
  336.8 3.6 fusion.130
  340.5 3.6 fusion.130
  345.1 211.7 %all-reduce.11.cloned.1.call-done = f32[128,256]{1,0:T(8,128)} async-done(((f32[128,256]{1,0:T(8,128)}), f32[128,256]{1,0:T(8,128)}) %all-reduce.11.cloned.1.call-update) | async-done | bytes 131088 | tf_op jit(solution)/shard_map/psum | solution.py:95
  559.9 31.0 %all-reduce.13.cloned.1.call-done = f32[256,256]{0,1:T(8,128)} async-done(((f32[256,256]{0,1:T(8,128)}), f32[256,256]{0,1:T(8,128)}) %all-reduce.13.cloned.1.call-update) | async-done | bytes 262160 | tf_op jit(solution)/shard_map/psum | solution.py:97
  598.6 11.7 %cholesky.240 = f32[128,128]{1,0:T(8,128)S(1)} custom-call(f32[128,128]{1,0:T(8,128)S(1)} %cholesky.276), custom_call_target="Cholesky" | custom-call | tf_op jit(solution)/shard_map/jit(cholesky)/cholesky | solution.py:14
  610.4 9.8 %custom-call.33 = f32[1,128,128]{1,2,0:T(8,128)S(1)} custom-call(f32[1,128,128]{2,1,0:T(8,128)S(1)} %get-tuple-element.199), custom_call_target="InvertDiagBlocksLowerTriangular" | custom-call | tf_op jit(solution)/shard_map/jit(cholesky)/cholesky | solution.py:14
  620.7 11.7 %cholesky.257 = f32[128,128]{1,0:T(8,128)S(1)} custom-call(f32[128,128]{1,0:T(8,128)S(1)} %convolution_subtract_fusion.6), custom_call_target="Cholesky" | custom-call | tf_op jit(solution)/shard_map/jit(cholesky)/cholesky | solution.py:14
  635.0 3.7 while.32
  638.7 19.9 %custom-call.34 = f32[2,128,128]{1,2,0:T(8,128)S(1)} custom-call(f32[2,128,128]{2,1,0:T(8,128)S(1)} %get-tuple-element.119), custom_call_target="InvertDiagBlocksLowerTriangular" | custom-call | tf_op jit(solution)/shard_map/jit(_cho_solve)/triangular_solve | solution.py:15
  660.3 7.2 while.29
  660.3 3.5 fusion.132
  663.9 3.5 fusion.132
  668.4 176.9 %all-reduce.15.cloned.1.call-done = f32[128,256]{1,0:T(8,128)} async-done(((f32[128,256]{1,0:T(8,128)}), f32[128,256]{1,0:T(8,128)}) %all-reduce.15.cloned.1.call-update) | async-done | bytes 131088 | tf_op jit(solution)/shard_map/psum | solution.py:114
  846.5 8.4 psum.47
  (141 shorter events, 51.8 us)
Async XLA Ops:
  7.2 115.3 %all-reduce.7.cloned.1.call-start = ((), (), s32[]{:S(2)}) async-start(), calls=%async_computation | async-start | bytes 524288 | tf_op jit(solution)/shard_map/psum | solution.py:69
  17.0 10.0 %copy-start.1 = (bf16[128,256]{1,0:T(8,128)(2,1)S(1)}, bf16[128,256]{1,0:T(8,128)(2,1)}, u32[]{:S(2)}) copy-start(bf16[128,256]{1,0:T(8,128)(2,1)} %param.16) | copy-start | bytes 196612
  17.1 21.0 %copy-start.3 = (bf16[128,256]{1,0:T(8,128)(2,1)S(1)}, bf16[128,256]{1,0:T(8,128)(2,1)}, u32[]{:S(2)}) copy-start(bf16[128,256]{1,0:T(8,128)(2,1)} %param.15) | copy-start | bytes 196612
  27.0 240.1 %all-reduce.9.cloned.1.call-start = ((), (), s32[]{:S(2)}) async-start(), calls=%async_computation.1 | async-start | bytes 524288 | tf_op jit(solution)/shard_map/psum | solution.py:74
  125.1 431.6 %all-reduce.11.cloned.1.call-start = ((), (), s32[]{:S(2)}) async-start(), calls=%async_computation.2 | async-start | bytes 262144 | tf_op jit(solution)/shard_map/psum | solution.py:95
  336.7 256.9 %copy-start = (f32[256,256]{0,1:T(8,128)S(1)}, f32[256,256]{0,1:T(8,128)}, u32[]{:S(2)}) copy-start(f32[256,256]{0,1:T(8,128)} %all-reduce.9.cloned.1.call-done) | copy-start | bytes 786436
  344.1 0.6 copy-start.5
  344.8 246.2 %all-reduce.13.cloned.1.call-start = ((), (), s32[]{:S(2)}) async-start(), calls=%async_computation.3 | async-start | bytes 524288 | tf_op jit(solution)/shard_map/psum | solution.py:97
  559.1 286.2 %all-reduce.15.cloned.1.call-start = ((), (), s32[]{:S(2)}) async-start(), calls=%async_computation.4 | async-start | bytes 262144 | tf_op jit(solution)/shard_map/psum | solution.py:114
  667.5 0.7 copy-start.4
  667.5 188.1 %copy-start.2 = (bf16[128,256]{1,0:T(8,128)(2,1)}, bf16[128,256]{1,0:T(8,128)(2,1)S(1)}, u32[]{:S(2)}) copy-start(bf16[128,256]{1,0:T(8,128)(2,1)S(1)} %get-tuple-element.465) | copy-start | bytes 196612
Sparse Core Ops, SparseCore 0:
  27.1 67.1 all-reduce.6
  125.2 141.8 all-reduce.8
  344.9 211.8 all-reduce.10
  559.2 31.7 all-reduce.12
  668.3 176.9 all-reduce.14
where the time goes:
time: 867 us; the launch traced here: 862 us
  waiting for transfers between devices  554 us (64%)
  other arithmetic  184 us (21%)
  matrix products  38.7 us (4%)
  local copies, waits for them, and re-layouts  38.7 us (4%)
  blocking collectives  25.7 us (3%)
  between operations  20.2 us (2%)
    psum x1, waiting for transfers between devices, on_device(): half_sums = lax.psum(running, ('neuron', 'trial'))  212 us
    psum x1, waiting for transfers between devices, on_device(): quarter_sums = lax.psum(running, ('neuron', 'tm'))  177 us
    psum x1, waiting for transfers between devices, on_device(): gram_sum = lax.psum(raw_gram(raw_rows), 'neuron')  135 us
    another operation x20, other arithmetic, normal_inverse(): lower_factor = jnp.linalg.cholesky(scaled)  103 us
    another operation x7, other arithmetic, normal_inverse(): return jax.scipy.linalg.cho_solve((lower_factor, True), identity)  59.9 us
    psum x1, waiting for transfers between devices, on_device(): gram_sum = lax.psum(raw_gram(raw_rows), 'tm')  31 us
  transfers between devices with their start and end apart: 5, of which 4 were waited for; matrix products, arithmetic and copies ran while one was open for 10% of the time, Pallas kernels for 0%

commit v1 on v0

--- a/solution.py
+++ b/solution.py
@@ -92,7 +92,7 @@
     running, unused = lax.scan(
         time_add_block, jnp.zeros((time_rows, rank_size), jnp.float32), (blocks, neuron_blocks)
     )
-    half_sums = lax.psum(running, ("neuron", "trial"))
+    half_sums = jnp.sum(lax.all_gather(running, ("neuron", "trial")), axis=0)
     raw_rows = apply_inverse(half_sums, inverse_time)
     gram_sum = lax.psum(raw_gram(raw_rows), "tm")
     time_local, gram_time = rescale(raw_rows, gram_sum, time_total)

time: 867 us -> 677 us (0.78)
  waiting for transfers between devices: 554 us -> 358 us
    psum x1 -> x0, waiting for transfers between devices: 212 us -> none  [on_device(): half_sums = lax.psum(running, ('neuron', 'trial'))]
    all_gather x0 -> x1, waiting for transfers between devices: none -> 85.4 us  [on_device(): half_sums = jnp.sum(lax.all_gather(running, ('neuron', 'trial')), axis=0)]
    psum x1, waiting for transfers between devices: 177 us -> 111 us  [on_device(): quarter_sums = lax.psum(running, ('neuron', 'tm'))]
  transfers between devices with their start and end apart: 5 -> 5, of which waited for: 4 -> 4; matrix products, arithmetic and copies ran while one was open for 10% -> 32% of each run, Pallas kernels for 0% -> 0%
where the time goes in v1:
time: 677 us; the launch traced here: 672 us
  waiting for transfers between devices  358 us (53%)
  other arithmetic  190 us (28%)
  local copies, waits for them, and re-layouts  39.5 us (6%)
  matrix products  37.8 us (6%)
  blocking collectives  25.7 us (4%)
  between operations  20.4 us (3%)
    psum x1, waiting for transfers between devices, on_device(): gram_sum = lax.psum(raw_gram(raw_rows), 'neuron')  135 us
    psum x1, waiting for transfers between devices, on_device(): quarter_sums = lax.psum(running, ('neuron', 'tm'))  111 us
    another operation x20, other arithmetic, normal_inverse(): lower_factor = jnp.linalg.cholesky(scaled)  103 us
    all_gather x1, waiting for transfers between devices, on_device(): half_sums = jnp.sum(lax.all_gather(running, ('neuron', 'trial')), axis=0)  85.4 us
    another operation x7, other arithmetic, normal_inverse(): return jax.scipy.linalg.cho_solve((lower_factor, True), identity)  59.8 us
    psum x1, waiting for transfers between devices, on_device(): gram_sum = lax.psum(raw_gram(raw_rows), 'tm')  26.9 us
    mul x2, other arithmetic, mask_tensor(): return shaped * block_mask.astype(jnp.bfloat16)[:, None, None, :]  14.4 us
    unnamed x17, local copies, waits for them, and re-layouts  14 us
  transfers between devices with their start and end apart: 5, of which 4 were waited for; matrix products, arithmetic and copies ran while one was open for 32% of the time, Pallas kernels for 0%

profile of v1, /device:TPU:1, one launch (start us, length us, event | category | flops | bytes accessed | tf_op | source)
XLA Modules:
  0.0 671.9 jit_solution(14465821176167481692)
XLA Ops:
  9.9 7.2 %broadcast_multiply_fusion.1 = bf16[256,128,128]{2,1,0:T(8,128)(2,1)} fusion(bf16[256,128,128]{2,1,0:T(8,128)(2,1)} %param.12, bf16[256,128]{1,0:T(8,128)(2,1)S(1)} %bitcast.177), kind=kLoop, calls=%fused_computation.37 | loop fusion | flops 4194304 | bytes 16842752 | tf_op jit(solution)/shard_map/mul | solution.py:49
  17.1 10.0 %fusion.28 = f32[256,256]{1,0:T(8,128)} fusion(f32[128,256]{1,0:T(8,128)S(1)} %convert_element_type.81, f32[128,256]{1,0:T(8,128)S(1)} %convert_element_type.80, bf16[256,128,128]{2,1,0:T(8,128)(2,1)} %broadcast_multiply_fusion.1), kind=kOutput, calls=%fused_computation.39 | convolution fusion | flops 2155872256 | bytes 8912896 | tf_op jit(solution)/shard_map/itk,tkr->ir/dot_general | solution.py:70
  27.1 11.0 %all_gather.13 = bf16[512,256]{1,0:T(8,128)(2,1)S(1)} all-gather(bf16[128,256]{1,0:T(8,128)(2,1)S(1)} %copy-done.2), channel_id=1, replica_groups=mesh['neuron'=32,'tm'=2,'trial'=4] {'trial'}, dimensions={0}, use_global_device_ids=true | all-gather | bytes 327680 | tf_op jit(solution)/shard_map/all_gather | solution.py:58
  38.1 6.3 all_gather.12
  44.5 11.9 %copy.27 = bf16[256,128,128]{1,2,0:T(8,128)(2,1)} copy(bf16[256,128,128]{2,1,0:T(8,128)(2,1)} %param.12) | data formatting | bytes 16777216 | tf_op args[0]
  60.8 11.7 %cholesky.172 = f32[128,128]{1,0:T(8,128)S(1)} custom-call(f32[128,128]{1,0:T(8,128)S(1)} %cholesky.270), custom_call_target="Cholesky" | custom-call | tf_op jit(solution)/shard_map/jit(cholesky)/cholesky | solution.py:14
  72.6 9.8 %custom-call.29 = f32[1,128,128]{1,2,0:T(8,128)S(1)} custom-call(f32[1,128,128]{2,1,0:T(8,128)S(1)} %get-tuple-element.207), custom_call_target="InvertDiagBlocksLowerTriangular" | custom-call | tf_op jit(solution)/shard_map/jit(cholesky)/cholesky | solution.py:14
  82.9 11.7 %cholesky.189 = f32[128,128]{1,0:T(8,128)S(1)} custom-call(f32[128,128]{1,0:T(8,128)S(1)} %convolution_subtract_fusion.8), custom_call_target="Cholesky" | custom-call | tf_op jit(solution)/shard_map/jit(cholesky)/cholesky | solution.py:14
  96.7 4.0 while.30
  100.7 19.9 %custom-call.30 = f32[2,128,128]{1,2,0:T(8,128)S(1)} custom-call(f32[2,128,128]{2,1,0:T(8,128)S(1)} %get-tuple-element.117), custom_call_target="InvertDiagBlocksLowerTriangular" | custom-call | tf_op jit(solution)/shard_map/jit(_cho_solve)/triangular_solve | solution.py:15
  125.2 7.2 %broadcast_multiply_fusion = bf16[2,128,128,128]{2,3,1,0:T(8,128)(2,1)} fusion(bf16[2,128,128,128]{2,3,1,0:T(8,128)(2,1)} %bitcast.174, bf16[2,128]{1,0:T(2,128)(2,1)S(1)} %fusion.31), kind=kLoop, calls=%fused_computation.36 | loop fusion | flops 4194304 | bytes 16777728 | tf_op jit(solution)/shard_map/mul | solution.py:49
  132.6 134.6 %all-reduce.8.cloned.1.call-done = f32[256,256]{0,1:T(8,128)} async-done(((f32[256,256]{0,1:T(8,128)}), f32[256,256]{0,1:T(8,128)}) %all-reduce.8.cloned.1.call-update) | async-done | bytes 262160 | tf_op jit(solution)/shard_map/psum | solution.py:74
  271.0 7.4 %while.28 = (s32[]{:T(128)}, f32[128,256]{1,0:T(8,128)S(1)}, bf16[2,128,128,128]{2,3,1,0:T(8,128)(2,1)}, bf16[2,128,256]{2,1,0:T(8,128)(2,1)S(1)}, bf16[128,256]{1,0:T(8,128)(2,1)S(1)}, /*index=5*/s32[]{:T(128)}, s32[]{:T(128)}) while((s32[]{:T(128)}, f32[128,256]{1,0:T(8,128)S(1)}, bf16[2,128,128,128]{2,3,1,0:T(8,128)(2,1)}, ...), condition=%wide.region_8.11_spmd.clone, body=%wide.region_7.10_spmd.clone.sunk | while | flops 1082261504 | bytes 5111911 | solution.py:92
  271.1 3.6 fusion.130
  274.7 3.6 fusion.130
  283.4 11.7 %cholesky.206 = f32[128,128]{1,0:T(8,128)S(1)} custom-call(f32[128,128]{1,0:T(8,128)S(1)} %cholesky.273), custom_call_target="Cholesky" | custom-call | tf_op jit(solution)/shard_map/jit(cholesky)/cholesky | solution.py:14
  295.2 9.8 %custom-call.31 = f32[1,128,128]{1,2,0:T(8,128)S(1)} custom-call(f32[1,128,128]{2,1,0:T(8,128)S(1)} %get-tuple-element.203), custom_call_target="InvertDiagBlocksLowerTriangular" | custom-call | tf_op jit(solution)/shard_map/jit(cholesky)/cholesky | solution.py:14
  305.5 11.7 %cholesky.223 = f32[128,128]{1,0:T(8,128)S(1)} custom-call(f32[128,128]{1,0:T(8,128)S(1)} %convolution_subtract_fusion.7), custom_call_target="Cholesky" | custom-call | tf_op jit(solution)/shard_map/jit(cholesky)/cholesky | solution.py:14
  319.7 3.8 while.31
  323.6 19.8 %custom-call.32 = f32[2,128,128]{1,2,0:T(8,128)S(1)} custom-call(f32[2,128,128]{2,1,0:T(8,128)S(1)} %get-tuple-element.118), custom_call_target="InvertDiagBlocksLowerTriangular" | custom-call | tf_op jit(solution)/shard_map/jit(_cho_solve)/triangular_solve | solution.py:15
  345.3 85.4 %all-gather.3.cloned.1.call-done = f32[16384,256]{1,0:T(8,128)} async-done(((f32[128,256]{1,0:T(8,128)}), f32[16384,256]{1,0:T(8,128)}) %all-gather.3.cloned.1.call-update) | async-done | bytes 16777232 | tf_op jit(solution)/shard_map/all_gather | solution.py:95
  430.7 6.8 %reduce_sum.46 = f32[128,256]{1,0:T(8,128)S(1)} reduce(f32[128,128,256]{2,1,0:T(8,128)} %bitcast.175, f32[]{:T(128)} %constant.118.clone.1), dimensions={0}, to_apply=%region_9.12 | reduce | flops 4161536 | bytes 16908292 | tf_op jit(solution)/shard_map/reduce_sum | solution.py:95
  439.8 26.9 %all-reduce.10.cloned.1.call-done = f32[256,256]{0,1:T(8,128)} async-done(((f32[256,256]{0,1:T(8,128)}), f32[256,256]{0,1:T(8,128)}) %all-reduce.10.cloned.1.call-update) | async-done | bytes 262160 | tf_op jit(solution)/shard_map/psum | solution.py:97
  469.3 7.2 %while.29 = (s32[]{:T(128)}, f32[128,256]{1,0:T(8,128)S(1)}, bf16[2,128,128,128]{2,3,1,0:T(8,128)(2,1)}, bf16[2,128,256]{2,1,0:T(8,128)(2,1)S(1)}, bf16[128,256]{1,0:T(8,128)(2,1)S(1)}, /*index=5*/s32[]{:T(128)}, s32[]{:T(128)}) while((s32[]{:T(128)}, f32[128,256]{1,0:T(8,128)S(1)}, bf16[2,128,128,128]{2,3,1,0:T(8,128)(2,1)}, ...), condition=%wide.region_13.16_spmd.clone, body=%wide.region_12.15_spmd.clone.sunk | while | flops 1082261504 | bytes 5111911 | solution.py:111
  469.3 3.6 fusion.132
  481.6 11.7 %cholesky.240 = f32[128,128]{1,0:T(8,128)S(1)} custom-call(f32[128,128]{1,0:T(8,128)S(1)} %cholesky.276), custom_call_target="Cholesky" | custom-call | tf_op jit(solution)/shard_map/jit(cholesky)/cholesky | solution.py:14
  493.4 9.8 %custom-call.33 = f32[1,128,128]{1,2,0:T(8,128)S(1)} custom-call(f32[1,128,128]{2,1,0:T(8,128)S(1)} %get-tuple-element.199), custom_call_target="InvertDiagBlocksLowerTriangular" | custom-call | tf_op jit(solution)/shard_map/jit(cholesky)/cholesky | solution.py:14
  503.7 11.7 %cholesky.257 = f32[128,128]{1,0:T(8,128)S(1)} custom-call(f32[128,128]{1,0:T(8,128)S(1)} %convolution_subtract_fusion.6), custom_call_target="Cholesky" | custom-call | tf_op jit(solution)/shard_map/jit(cholesky)/cholesky | solution.py:14
  518.1 4.1 while.32
  522.2 19.9 %custom-call.34 = f32[2,128,128]{1,2,0:T(8,128)S(1)} custom-call(f32[2,128,128]{2,1,0:T(8,128)S(1)} %get-tuple-element.119), custom_call_target="InvertDiagBlocksLowerTriangular" | custom-call | tf_op jit(solution)/shard_map/jit(_cho_solve)/triangular_solve | solution.py:15
  544.0 110.9 %all-reduce.12.cloned.1.call-done = f32[128,256]{1,0:T(8,128)} async-done(((f32[128,256]{1,0:T(8,128)}), f32[128,256]{1,0:T(8,128)}) %all-reduce.12.cloned.1.call-update) | async-done | bytes 131088 | tf_op jit(solution)/shard_map/psum | solution.py:114
  656.1 8.4 %psum.39 = f32[256]{0:T(256)S(1)} all-reduce(f32[256]{0:T(256)S(1)} %get-tuple-element.216), channel_id=1, replica_groups=mesh['neuron'=32,'tm'=2,'trial'=4] {'trial'}, use_global_device_ids=true, to_apply=%region_17.20 | all-reduce | flops 256 | bytes 2048 | tf_op jit(solution)/shard_map/psum | solution.py:116
  (144 shorter events, 54.4 us)
Async XLA Ops:
  7.2 115.3 %all-reduce.6.cloned.1.call-start = ((), (), s32[]{:S(2)}) async-start(), calls=%async_computation | async-start | bytes 524288 | tf_op jit(solution)/shard_map/psum | solution.py:69
  17.0 10.0 %copy-start.2 = (bf16[128,256]{1,0:T(8,128)(2,1)S(1)}, bf16[128,256]{1,0:T(8,128)(2,1)}, u32[]{:S(2)}) copy-start(bf16[128,256]{1,0:T(8,128)(2,1)} %param.16) | copy-start | bytes 196612
  17.1 21.1 %copy-start.4 = (bf16[128,256]{1,0:T(8,128)(2,1)S(1)}, bf16[128,256]{1,0:T(8,128)(2,1)}, u32[]{:S(2)}) copy-start(bf16[128,256]{1,0:T(8,128)(2,1)} %param.15) | copy-start | bytes 196612
  27.0 240.1 %all-reduce.8.cloned.1.call-start = ((), (), s32[]{:S(2)}) async-start(), calls=%async_computation.1 | async-start | bytes 524288 | tf_op jit(solution)/shard_map/psum | solution.py:74
  125.2 305.5 %all-gather.3.cloned.1.call-start = ((), (), s32[]{:S(2)}) async-start(), calls=%async_computation.4 | async-start | bytes 16908288 | tf_op jit(solution)/shard_map/all_gather | solution.py:95
  278.4 0.6 copy-start.6
  279.0 187.6 %all-reduce.10.cloned.1.call-start = ((), (), s32[]{:S(2)}) async-start(), calls=%async_computation.2 | async-start | bytes 524288 | tf_op jit(solution)/shard_map/psum | solution.py:97
  438.9 216.0 %all-reduce.12.cloned.1.call-start = ((), (), s32[]{:S(2)}) async-start(), calls=%async_computation.3 | async-start | bytes 262144 | tf_op jit(solution)/shard_map/psum | solution.py:114
  469.3 7.9 %copy-start = (f32[256,256]{0,1:T(8,128)S(1)}, f32[256,256]{0,1:T(8,128)}, u32[]{:S(2)}) copy-start(f32[256,256]{0,1:T(8,128)} %all-reduce.8.cloned.1.call-done) | copy-start | bytes 786436
  469.3 7.9 %copy-start.1 = (f32[256,256]{0,1:T(8,128)S(1)}, f32[256,256]{0,1:T(8,128)}, u32[]{:S(2)}) copy-start(f32[256,256]{0,1:T(8,128)} %all-reduce.10.cloned.1.call-done) | copy-start | bytes 786436
  476.5 0.7 copy-start.5
  476.5 188.6 %copy-start.3 = (bf16[128,256]{1,0:T(8,128)(2,1)}, bf16[128,256]{1,0:T(8,128)(2,1)S(1)}, u32[]{:S(2)}) copy-start(bf16[128,256]{1,0:T(8,128)(2,1)S(1)} %get-tuple-element.466) | copy-start | bytes 196612
Sparse Core Ops, SparseCore 0:
  27.2 67.2 all-reduce.5
  125.3 141.8 all-reduce.7
  279.2 151.4 all-gather.2
  439.0 27.5 all-reduce.9
  477.3 177.4 all-reduce.11
